TPU v7x, 32 devices: a whole 2x2x4 slice. The times are simulated.
32 devices in a mesh: groups: 2 (over y), section: 4 (over z), seq: 4 (over x, core).
Axes of the slice: x: 2, y: 2, z: 4, core: 2. Of those that a mesh axis runs over, the one named last changes fastest.
Arguments:
- incoming_states: bfloat16 [1536, 3072], P('groups', 'seq'), parts along dimension 0, may hold values from -6 to 6
- transit_states: bfloat16 [4, 512, 3072], P('section', 'groups', 'seq'), parts along dimension 1, may hold values from -6 to 6
- patch_sizes_list: int32 [8], P('groups'), parts along dimension 0, may hold values from 1 to 256, 768 in all
- outdated_lookups: bfloat16 [4, 16, 1536, 128], P('section', 'seq', 'groups'), parts along dimension 2, may hold values from -6 to 6
- outdated_contents: bfloat16 [4, 16, 1536, 128], P('section', 'seq', 'groups'), parts along dimension 2, may hold values from -6 to 6
- attention_projection: bfloat16 [4, 3072, 6144], P('section', None, 'seq'), may hold values from -0.109375 to 0.109375
- exit_projection: bfloat16 [4, 2048, 3072], P('section', None, 'seq'), may hold values from -0.125 to 0.125
- shift_and_scale: float32 [4, 2, 3072], P('section'), may hold values from -3 to 3
- branch_gates: float32 [4, 3072], P('section', 'seq'), may hold values from -4 to 4
Outputs:
- section_out: bfloat16 [4, 4, 512, 3072], P(None, 'section', 'groups', 'seq'), parts along dimension 2
There are 2 independent parts, one for each index of `groups`. A program takes and returns all parts, laid end to end along the dimension named above; an argument that names none is the same for every part. Nothing has to cross between parts.
Inputs may be any that keep to these rules, and one draw needn't show every extreme that they name: `patch_sizes_list`: the 4 counts sum to 768; the largest equals 256.
All inputs are finite; a program needn't handle non-finite values.
Results may differ from a plain program's by a relative error of at most 0.005.
Values may be sent and summed in bfloat16 or wider, within the bound.
No kernel may reach another device: no remote copies, remote signals or barrier semaphores. Data moves between devices by JAX's collectives and lax.ppermute only.
A program may use at most 128 MiB of HBM per device.

v0:
```python
import jax
import jax.numpy as jnp
from jax import lax
from jax.sharding import PartitionSpec as P

epsilon = 1e-06


def passed_along(value, axis, steps):
    count = lax.axis_size(axis)
    leading, last = (max(0, -steps), min(count, count - steps))
    return lax.ppermute(value, axis, [(source, source + steps) for source in range(leading, last)])


def layer_norm(values):
    row_mean = jnp.mean(values, axis=-1, keepdims=True)
    centred = values - row_mean
    spread = jnp.mean(centred * centred, axis=-1, keepdims=True)
    return centred * lax.rsqrt(spread + epsilon)


def rms_norm(values):
    return values * lax.rsqrt(jnp.mean(values * values, axis=-1, keepdims=True) + epsilon)


def pick_entry(vector, position):
    return jnp.sum(jnp.where(jnp.arange(vector.shape[0]) == position, vector, 0))


def run_block(
    full_rows,
    own_rows,
    live_rows,
    patch_start,
    key_cache,
    value_cache,
    qkv_weights,
    shift_scale,
    gating_here,
    project,
):
    biggest_patch_span = full_rows.shape[0]
    heads_here = key_cache.shape[0]
    head_dim = key_cache.shape[2]
    seq_len = key_cache.shape[1] - biggest_patch_span
    shaped = (
        layer_norm(full_rows.astype(jnp.float32)) * (1.0 + shift_scale[1]) + shift_scale[0]
    ).astype(jnp.bfloat16)
    mixed = jnp.dot(shaped, qkv_weights, preferred_element_type=jnp.float32).reshape(
        biggest_patch_span, heads_here, 3, head_dim
    )
    queries = rms_norm(mixed[:, :, 0]).astype(jnp.bfloat16)
    fresh_keys = jnp.transpose(rms_norm(mixed[:, :, 1]).astype(jnp.bfloat16), (1, 0, 2))
    fresh_values = jnp.transpose(mixed[:, :, 2].astype(jnp.bfloat16), (1, 0, 2))
    mask = live_rows[None, :, None]
    window = lax.dynamic_slice_in_dim(key_cache, patch_start, biggest_patch_span, 1)
    key_cache = lax.dynamic_update_slice_in_dim(
        key_cache, jnp.where(mask, fresh_keys, window), patch_start, 1
    )
    window = lax.dynamic_slice_in_dim(value_cache, patch_start, biggest_patch_span, 1)
    value_cache = lax.dynamic_update_slice_in_dim(
        value_cache, jnp.where(mask, fresh_values, window), patch_start, 1
    )
    scores = jnp.einsum(
        "qhd,hkd->hqk", queries, key_cache[:, :seq_len], preferred_element_type=jnp.float32
    ) * head_dim ** (-0.5)
    expos = jnp.exp(scores)
    weights = (expos / jnp.sum(expos, axis=-1, keepdims=True)).astype(jnp.bfloat16)
    attended = jnp.einsum(
        "hqk,hkd->qhd", weights, value_cache[:, :seq_len], preferred_element_type=jnp.float32
    ).astype(jnp.bfloat16)
    head_rows = attended.reshape(biggest_patch_span, heads_here * head_dim)
    projected = project(head_rows)
    updated = own_rows.astype(jnp.float32) + gating_here * projected
    updated = jnp.where(live_rows[:, None], updated, 0.0).astype(jnp.bfloat16)
    return (updated, key_cache, value_cache)


def shards(
    incoming_states,
    transit_states,
    patch_sizes_list,
    outdated_lookups,
    outdated_contents,
    attention_projection,
    exit_projection,
    shift_and_scale,
    branch_gates,
):
    section_index = lax.axis_index("section")
    patches = patch_sizes_list.shape[0]
    biggest_patch_span = transit_states.shape[1]
    columns = incoming_states.shape[1]
    heads_here = outdated_lookups.shape[1]
    head_dim = outdated_lookups.shape[3]
    starts = jnp.cumsum(patch_sizes_list) - patch_sizes_list
    padding = jnp.zeros((heads_here, biggest_patch_span, head_dim), jnp.bfloat16)
    key_cache = jnp.concatenate([outdated_lookups[0], padding], axis=1)
    value_cache = jnp.concatenate([outdated_contents[0], padding], axis=1)
    qkv_weights = attention_projection[0]
    out_weights = exit_projection[0]
    shift_scale = shift_and_scale[0]
    gating_here = branch_gates[0]
    row_numbers = jnp.arange(biggest_patch_span)

    def gather_heads(head_rows):
        every_head = lax.all_gather(head_rows, "seq", axis=1, tiled=True)
        return jnp.dot(every_head, out_weights, preferred_element_type=jnp.float32)

    results = []
    entering_ext = jnp.concatenate(
        [incoming_states, jnp.zeros((biggest_patch_span, columns), jnp.bfloat16)], axis=0
    )
    earlier_result = transit_states[0]
    for turn_number in range(patches):
        patch_index = jnp.remainder(turn_number - section_index, patches)
        patch_count = pick_entry(patch_sizes_list, patch_index)
        patch_start = pick_entry(starts, patch_index)
        live_rows = row_numbers < patch_count
        entry_patch = lax.dynamic_slice_in_dim(
            entering_ext, starts[turn_number], biggest_patch_span, 0
        )
        own_rows = jnp.where(section_index == 0, entry_patch, earlier_result)
        own_rows = jnp.where(live_rows[:, None], own_rows, jnp.zeros_like(own_rows))
        full_rows = lax.all_gather(own_rows, "seq", axis=1, tiled=True)
        updated, key_cache, value_cache = run_block(
            full_rows,
            own_rows,
            live_rows,
            patch_start,
            key_cache,
            value_cache,
            qkv_weights,
            shift_scale,
            gating_here,
            gather_heads,
        )
        results.append(updated)
        if turn_number + 1 < patches:
            earlier_result = passed_along(updated, "section", 1)
    return jnp.stack(results)[:, None]


def solution(mesh):
    return jax.shard_map(
        shards,
        mesh=mesh,
        in_specs=(
            P("groups", "seq"),
            P("section", "groups", "seq"),
            P("groups"),
            P("section", "seq", "groups", None),
            P("section", "seq", "groups", None),
            P("section", None, "seq"),
            P("section", None, "seq"),
            P("section", None, None),
            P("section", "seq"),
        ),
        out_specs=P(None, "section", "groups", "seq"),
        check_vma=False,
    )
```

profile of v0, /device:TPU:0, one launch (start us, length us, event | category | flops | bytes accessed | tf_op | source)
XLA Modules:
  0.0 327.7 jit_solution(2446914256059857910)
XLA Ops:
  15.7 2.3 copy.35
  18.1 2.3 copy.32
  24.9 12.7 %copy.33 = bf16[1,3072,1536]{1,2,0:T(8,128)(2,1)} copy(bf16[1,3072,1536]{2,1,0:T(8,128)(2,1)} %param.14) | data formatting | bytes 18874368 | tf_op args[5]
  42.2 5.7 %fusion.37 = f32[256,4,3,128]{0,3,2,1:T(8,128)S(1)} fusion(bf16[4,3,128,3072]{3,2,1,0:T(8,128)(2,1)} %bitcast.213, bf16[256,3072]{1,0:T(8,128)(2,1)S(1)} %copy-done.3, f32[3072]{0:T(1024)S(1)} %bitcast.229, f32[3072]{0:T(1024)S(1)} %bitcast.225, f32[256]{0:T(256)S(1)} %add_rsqrt_fusion.11, f32[256]{0:T(256)S(1)} %broadcast_multiply_fusion.3), kind=kOutput, calls=%fused_computation.57 | convolution fusion | flops 2420637696 | bytes 12609536 | tf_op jit(solution)/shard_map/dot_general | solution.py:49
  49.1 3.5 %dynamic_update_slice.24 = bf16[4,1024,128]{1,2,0:T(8,128)(2,1)} dynamic-update-slice(bf16[4,1024,128]{1,2,0:T(8,128)(2,1)} %concatenate.10, bf16[4,256,128]{1,2,0:T(8,128)(2,1)} %get-tuple-element.28, s32[]{:T(128)} %constant.58.clone.1, s32[]{:T(128)S(6)} %select_n.158, s32[]{:T(128)} %constant.58.clone.1) | dynamic-update-slice | bytes 524292 | tf_op jit(solution)/shard_map/dynamic_update_slice | solution.py:61
  52.6 3.4 %dynamic_update_slice.25 = bf16[4,1024,128]{1,2,0:T(8,128)(2,1)} dynamic-update-slice(bf16[4,1024,128]{1,2,0:T(8,128)(2,1)} %concatenate.11, bf16[4,256,128]{1,2,0:T(8,128)(2,1)S(1)} %get-tuple-element.29, s32[]{:T(128)} %constant.58.clone.1, s32[]{:T(128)S(6)} %select_n.158, s32[]{:T(128)} %constant.58.clone.1) | dynamic-update-slice | bytes 524292 | tf_op jit(solution)/shard_map/dynamic_update_slice | solution.py:57
  60.5 19.7 %all-gather.11.cloned.1.call-done = bf16[256,2048]{0,1:T(8,128)(2,1)} async-done(((bf16[256,512]{0,1:T(8,128)(2,1)}), bf16[256,2048]{0,1:T(8,128)(2,1)}) %all-gather.11.cloned.1.call-update) | async-done | bytes 1048592 | tf_op jit(solution)/shard_map/all_gather | solution.py:107
  80.2 3.0 fusion.86
  83.3 3.4 %collective-permute-start = (bf16[256,768]{1,0:T(8,128)(2,1)}, bf16[256,768]{1,0:T(8,128)(2,1)S(1)}, u32[]{:S(2)}, u32[]{:S(2)}) collective-permute-start(bf16[256,768]{1,0:T(8,128)(2,1)} %fusion.86), channel_id=1, source_target_pairs={{0,4},{4,8},{8,12},{1,5},{5,9},{9,13},{2,6},{6,10},{10,14},{3,7},{... | collective-permute-start | bytes 1179656 | tf_op jit(solution)/shard_map/ppermute | solution.py:12
  89.4 6.4 %collective-permute-done = bf16[256,768]{1,0:T(8,128)(2,1)S(1)} collective-permute-done((bf16[256,768]{1,0:T(8,128)(2,1)}, bf16[256,768]{1,0:T(8,128)(2,1)S(1)}, u32[]{:S(2)}, u32[]{:S(2)}) %collective-permute-start) | collective-permute-done | bytes 393248 | tf_op jit(solution)/shard_map/ppermute | solution.py:12
  99.8 18.7 %all-gather.13.cloned.1.call-done = bf16[256,3072]{1,0:T(8,128)(2,1)} async-done(((bf16[256,768]{1,0:T(8,128)(2,1)}), bf16[256,3072]{1,0:T(8,128)(2,1)}) %all-gather.13.cloned.1.call-update) | async-done | bytes 1572880 | tf_op jit(solution)/shard_map/all_gather | solution.py:125
  122.3 5.6 %fusion.40 = f32[256,4,3,128]{0,3,2,1:T(8,128)S(1)} fusion(bf16[4,3,128,3072]{3,2,1,0:T(8,128)(2,1)} %bitcast.214, bf16[256,3072]{1,0:T(8,128)(2,1)S(1)} %copy-done.5, f32[256]{0:T(256)S(1)} %add_rsqrt_fusion.10, f32[256]{0:T(256)S(1)} %broadcast_multiply_fusion.2, f32[3072]{0:T(1024)S(1)} %bitcast.230, f32[3072]{0:T(1024)S(1)} %bitcast.226), kind=kOutput, calls=%fused_computation.59 | convolution fusion | flops 2420637696 | bytes 12609536 | tf_op jit(solution)/shard_map/dot_general | solution.py:49
  131.1 3.9 %dynamic_update_slice.26 = bf16[4,1024,128]{1,2,0:T(8,128)(2,1)} dynamic-update-slice(bf16[4,1024,128]{1,2,0:T(8,128)(2,1)} %dynamic_update_slice.24, bf16[4,256,128]{1,2,0:T(8,128)(2,1)} %get-tuple-element.26, s32[]{:T(128)} %constant.58.clone.1, s32[]{:T(128)S(6)} %select_n.168, s32[]{:T(128)} %constant.58.clone.1) | dynamic-update-slice | bytes 524292 | tf_op jit(solution)/shard_map/dynamic_update_slice | solution.py:61
  135.0 3.8 %dynamic_update_slice.27 = bf16[4,1024,128]{1,2,0:T(8,128)(2,1)} dynamic-update-slice(bf16[4,1024,128]{1,2,0:T(8,128)(2,1)} %dynamic_update_slice.25, bf16[4,256,128]{1,2,0:T(8,128)(2,1)S(1)} %get-tuple-element.27, s32[]{:T(128)} %constant.58.clone.1, s32[]{:T(128)S(6)} %select_n.168, s32[]{:T(128)} %constant.58.clone.1) | dynamic-update-slice | bytes 524292 | tf_op jit(solution)/shard_map/dynamic_update_slice | solution.py:57
  142.6 16.8 %all-gather.15.cloned.1.call-done = bf16[256,2048]{0,1:T(8,128)(2,1)} async-done(((bf16[256,512]{0,1:T(8,128)(2,1)}), bf16[256,2048]{0,1:T(8,128)(2,1)}) %all-gather.15.cloned.1.call-update) | async-done | bytes 1048592 | tf_op jit(solution)/shard_map/all_gather | solution.py:107
  159.5 3.0 select_convert_fusion.2
  162.5 3.4 %collective-permute-start.1 = (bf16[256,768]{1,0:T(8,128)(2,1)}, bf16[256,768]{1,0:T(8,128)(2,1)S(1)}, u32[]{:S(2)}, u32[]{:S(2)}) collective-permute-start(bf16[256,768]{1,0:T(8,128)(2,1)} %select_convert_fusion.2), channel_id=1, source_target_pairs={{0,4},{4,8},{8,12},{1,5},{5,9},{9,13},{2,6},{6,10},{10,14},{3,7},{... | collective-permute-start | bytes 1179656 | tf_op jit(solution)/shard_map/ppermute | solution.py:12
  168.6 6.3 %collective-permute-done.1 = bf16[256,768]{1,0:T(8,128)(2,1)S(1)} collective-permute-done((bf16[256,768]{1,0:T(8,128)(2,1)}, bf16[256,768]{1,0:T(8,128)(2,1)S(1)}, u32[]{:S(2)}, u32[]{:S(2)}) %collective-permute-start.1) | collective-permute-done | bytes 393248 | tf_op jit(solution)/shard_map/ppermute | solution.py:12
  179.0 18.6 %all-gather.17.cloned.1.call-done = bf16[256,3072]{1,0:T(8,128)(2,1)} async-done(((bf16[256,768]{1,0:T(8,128)(2,1)}), bf16[256,3072]{1,0:T(8,128)(2,1)}) %all-gather.17.cloned.1.call-update) | async-done | bytes 1572880 | tf_op jit(solution)/shard_map/all_gather | solution.py:125
  201.4 5.6 %fusion.43 = f32[256,4,3,128]{0,3,2,1:T(8,128)S(1)} fusion(bf16[4,3,128,3072]{3,2,1,0:T(8,128)(2,1)} %bitcast.215, bf16[256,3072]{1,0:T(8,128)(2,1)S(1)} %copy-done.6, f32[256]{0:T(256)S(1)} %add_rsqrt_fusion.9, f32[256]{0:T(256)S(1)} %broadcast_multiply_fusion.1, f32[3072]{0:T(1024)S(1)} %bitcast.231, f32[3072]{0:T(1024)S(1)} %bitcast.227), kind=kOutput, calls=%fused_computation.61 | convolution fusion | flops 2420637696 | bytes 12609536 | tf_op jit(solution)/shard_map/dot_general | solution.py:49
  210.3 3.9 %dynamic_update_slice.28 = bf16[4,1024,128]{1,2,0:T(8,128)(2,1)} dynamic-update-slice(bf16[4,1024,128]{1,2,0:T(8,128)(2,1)} %dynamic_update_slice.26, bf16[4,256,128]{1,2,0:T(8,128)(2,1)} %get-tuple-element.24, s32[]{:T(128)} %constant.58.clone.1, s32[]{:T(128)S(6)} %select_n.178, s32[]{:T(128)} %constant.58.clone.1) | dynamic-update-slice | bytes 524292 | tf_op jit(solution)/shard_map/dynamic_update_slice | solution.py:61
  214.2 3.8 %dynamic_update_slice.29 = bf16[4,1024,128]{1,2,0:T(8,128)(2,1)} dynamic-update-slice(bf16[4,1024,128]{1,2,0:T(8,128)(2,1)} %dynamic_update_slice.27, bf16[4,256,128]{1,2,0:T(8,128)(2,1)S(1)} %get-tuple-element.25, s32[]{:T(128)} %constant.58.clone.1, s32[]{:T(128)S(6)} %select_n.178, s32[]{:T(128)} %constant.58.clone.1) | dynamic-update-slice | bytes 524292 | tf_op jit(solution)/shard_map/dynamic_update_slice | solution.py:57
  221.8 15.9 %all-gather.19.cloned.1.call-done = bf16[256,2048]{0,1:T(8,128)(2,1)} async-done(((bf16[256,512]{0,1:T(8,128)(2,1)}), bf16[256,2048]{0,1:T(8,128)(2,1)}) %all-gather.19.cloned.1.call-update) | async-done | bytes 1048592 | tf_op jit(solution)/shard_map/all_gather | solution.py:107
  237.7 3.0 select_convert_fusion.1
  240.7 3.6 %collective-permute-start.2 = (bf16[256,768]{1,0:T(8,128)(2,1)}, bf16[256,768]{1,0:T(8,128)(2,1)S(1)}, u32[]{:S(2)}, u32[]{:S(2)}) collective-permute-start(bf16[256,768]{1,0:T(8,128)(2,1)} %select_convert_fusion.1), channel_id=1, source_target_pairs={{0,4},{4,8},{8,12},{1,5},{5,9},{9,13},{2,6},{6,10},{10,14},{3,7},{... | collective-permute-start | bytes 1179656 | tf_op jit(solution)/shard_map/ppermute | solution.py:12
  246.8 6.3 %collective-permute-done.2 = bf16[256,768]{1,0:T(8,128)(2,1)S(1)} collective-permute-done((bf16[256,768]{1,0:T(8,128)(2,1)}, bf16[256,768]{1,0:T(8,128)(2,1)S(1)}, u32[]{:S(2)}, u32[]{:S(2)}) %collective-permute-start.2) | collective-permute-done | bytes 393248 | tf_op jit(solution)/shard_map/ppermute | solution.py:12
  257.0 18.9 %all-gather.21.cloned.1.call-done = bf16[256,3072]{1,0:T(8,128)(2,1)} async-done(((bf16[256,768]{1,0:T(8,128)(2,1)}), bf16[256,3072]{1,0:T(8,128)(2,1)}) %all-gather.21.cloned.1.call-update) | async-done | bytes 1572880 | tf_op jit(solution)/shard_map/all_gather | solution.py:125
  279.7 5.6 %fusion.46 = f32[256,4,3,128]{0,3,2,1:T(8,128)S(1)} fusion(bf16[4,3,128,3072]{3,2,1,0:T(8,128)(2,1)} %bitcast.216, bf16[256,3072]{1,0:T(8,128)(2,1)S(1)} %copy-done.4, f32[256]{0:T(256)S(1)} %add_rsqrt_fusion.8, f32[256]{0:T(256)S(1)} %broadcast_multiply_fusion, f32[3072]{0:T(1024)S(1)} %bitcast.232, f32[3072]{0:T(1024)S(1)} %bitcast.228), kind=kOutput, calls=%fused_computation.63 | convolution fusion | flops 2420637696 | bytes 12609536 | tf_op jit(solution)/shard_map/dot_general | solution.py:49
  288.5 3.9 %dynamic_update_slice.30 = bf16[4,1024,128]{1,2,0:T(8,128)(2,1)} dynamic-update-slice(bf16[4,1024,128]{1,2,0:T(8,128)(2,1)} %dynamic_update_slice.28, bf16[4,256,128]{1,2,0:T(8,128)(2,1)} %get-tuple-element.18, s32[]{:T(128)} %constant.58.clone.1, s32[]{:T(128)S(6)} %select_n.188, s32[]{:T(128)} %constant.58.clone.1) | dynamic-update-slice | bytes 524292 | tf_op jit(solution)/shard_map/dynamic_update_slice | solution.py:61
  292.4 3.8 %dynamic_update_slice.31 = bf16[4,1024,128]{1,2,0:T(8,128)(2,1)} dynamic-update-slice(bf16[4,1024,128]{1,2,0:T(8,128)(2,1)} %dynamic_update_slice.29, bf16[4,256,128]{1,2,0:T(8,128)(2,1)S(1)} %get-tuple-element.19, s32[]{:T(128)} %constant.58.clone.1, s32[]{:T(128)S(6)} %select_n.188, s32[]{:T(128)} %constant.58.clone.1) | dynamic-update-slice | bytes 524292 | tf_op jit(solution)/shard_map/dynamic_update_slice | solution.py:57
  299.9 16.2 %all-gather.23.cloned.1.call-done = bf16[256,2048]{0,1:T(8,128)(2,1)} async-done(((bf16[256,512]{0,1:T(8,128)(2,1)}), bf16[256,2048]{0,1:T(8,128)(2,1)}) %all-gather.23.cloned.1.call-update) | async-done | bytes 1048592 | tf_op jit(solution)/shard_map/all_gather | solution.py:107
  318.3 2.6 maximum_bitcast_fusion
  (139 shorter events, 62.5 us)
Async XLA Ops:
  6.5 73.7 %copy-start = (bf16[1,2048,768]{2,1,0:T(8,128)(2,1)S(1)}, bf16[1,2048,768]{2,1,0:T(8,128)(2,1)}, u32[]{:S(2)}) copy-start(bf16[1,2048,768]{2,1,0:T(8,128)(2,1)} %param.15) | copy-start | bytes 9437188
  6.5 31.8 %all-gather.9.cloned.1.call-start = ((), (), s32[]{:S(2)}) async-start(), calls=%async_computation | async-start | bytes 1966080 | tf_op jit(solution)/shard_map/all_gather | solution.py:125
  9.7 38.4 %copy-start.31 = (pred[256]{0:T(512)(128)(4,1)}, pred[256]{0:T(512)(128)(4,1)S(1)}, u32[]{:S(2)}) copy-start(pred[256]{0:T(512)(128)(4,1)S(1)} %iota_compare_fusion.3) | copy-start | bytes 772
  14.4 65.8 %all-gather.11.cloned.1.call-start = ((), (), s32[]{:S(2)}) async-start(), calls=%async_computation.1 | async-start | bytes 1310720 | tf_op jit(solution)/shard_map/all_gather | solution.py:107
  24.9 13.4 %copy-start.19 = (f32[1,2,3072]{2,1,0:T(2,128)S(1)}, f32[1,2,3072]{2,1,0:T(2,128)}, u32[]{:S(2)}) copy-start(f32[1,2,3072]{2,1,0:T(2,128)} %param.16) | copy-start | bytes 73732
  38.3 9.6 %copy-start.20 = (f32[1,1,3072]{2,1,0:T(1,128)}, f32[1,1,3072]{2,1,0:T(1,128)S(1)}, u32[]{:S(2)}) copy-start(f32[1,1,3072]{2,1,0:T(1,128)S(1)} %get-tuple-element.17) | copy-start | bytes 36868
  42.2 5.9 %copy-start.1 = (bf16[1,4,768,128]{2,3,1,0:T(8,128)(2,1)S(1)}, bf16[1,4,768,128]{2,3,1,0:T(8,128)(2,1)}, u32[]{:S(2)}) copy-start(bf16[1,4,768,128]{2,3,1,0:T(8,128)(2,1)} %copy.35) | copy-start | bytes 2359300
  42.2 5.9 %copy-start.2 = (bf16[1,4,768,128]{2,3,1,0:T(8,128)(2,1)S(1)}, bf16[1,4,768,128]{2,3,1,0:T(8,128)(2,1)}, u32[]{:S(2)}) copy-start(bf16[1,4,768,128]{2,3,1,0:T(8,128)(2,1)} %copy.32) | copy-start | bytes 2359300
  58.2 22.1 %copy-start.15 = (bf16[256,768]{1,0:T(8,128)(2,1)S(1)}, bf16[256,768]{1,0:T(8,128)(2,1)}, u32[]{:S(2)}) copy-start(bf16[256,768]{1,0:T(8,128)(2,1)} %fusion.107) | copy-start | bytes 1179652
  59.7 58.7 %all-gather.13.cloned.1.call-start = ((), (), s32[]{:S(2)}) async-start(), calls=%async_computation.2 | async-start | bytes 1966080 | tf_op jit(solution)/shard_map/all_gather | solution.py:125
  83.3 12.5 %collective-permute-start = (bf16[256,768]{1,0:T(8,128)(2,1)}, bf16[256,768]{1,0:T(8,128)(2,1)S(1)}, u32[]{:S(2)}, u32[]{:S(2)}) collective-permute-start(bf16[256,768]{1,0:T(8,128)(2,1)} %fusion.86), channel_id=1, source_target_pairs={{0,4},{4,8},{8,12},{1,5},{5,9},{9,13},{2,6},{6,10},{10,14},{3,7},{... | collective-permute-start | bytes 1179656 | tf_op jit(solution)/shard_map/ppermute | solution.py:12
  89.4 6.4 %copy-start.27 = (pred[256]{0:T(512)(128)(4,1)}, pred[256]{0:T(512)(128)(4,1)S(1)}, u32[]{:S(2)}) copy-start(pred[256]{0:T(512)(128)(4,1)S(1)} %iota_compare_fusion.2) | copy-start | bytes 772
  97.7 24.5 %copy-start.21 = (f32[1,1,3072]{2,1,0:T(1,128)S(1)}, f32[1,1,3072]{2,1,0:T(1,128)}, u32[]{:S(2)}) copy-start(f32[1,1,3072]{2,1,0:T(1,128)} %copy-done.20) | copy-start | bytes 36868
  97.7 61.7 %all-gather.15.cloned.1.call-start = ((), (), s32[]{:S(2)}) async-start(), calls=%async_computation.3 | async-start | bytes 1310720 | tf_op jit(solution)/shard_map/all_gather | solution.py:107
  118.4 3.8 %copy-start.5 = (bf16[256,3072]{1,0:T(8,128)(2,1)S(1)}, bf16[256,3072]{1,0:T(8,128)(2,1)}, u32[]{:S(2)}) copy-start(bf16[256,3072]{1,0:T(8,128)(2,1)} %all-gather.13.cloned.1.call-done) | copy-start | bytes 4718596
  122.2 6.7 %copy-start.28 = (pred[256]{0:T(512)(128)(4,1)S(1)}, pred[256]{0:T(512)(128)(4,1)}, u32[]{:S(2)}) copy-start(pred[256]{0:T(512)(128)(4,1)} %copy-done.27) | copy-start | bytes 772
  141.0 18.4 %copy-start.17 = (bf16[256,768]{1,0:T(8,128)(2,1)S(1)}, bf16[256,768]{1,0:T(8,128)(2,1)}, u32[]{:S(2)}) copy-start(bf16[256,768]{1,0:T(8,128)(2,1)} %fusion.109) | copy-start | bytes 1179652
  142.6 55.1 %all-gather.17.cloned.1.call-start = ((), (), s32[]{:S(2)}) async-start(), calls=%async_computation.4 | async-start | bytes 1966080 | tf_op jit(solution)/shard_map/all_gather | solution.py:125
  162.5 12.5 %collective-permute-start.1 = (bf16[256,768]{1,0:T(8,128)(2,1)}, bf16[256,768]{1,0:T(8,128)(2,1)S(1)}, u32[]{:S(2)}, u32[]{:S(2)}) collective-permute-start(bf16[256,768]{1,0:T(8,128)(2,1)} %select_convert_fusion.2), channel_id=1, source_target_pairs={{0,4},{4,8},{8,12},{1,5},{5,9},{9,13},{2,6},{6,10},{10,14},{3,7},{... | collective-permute-start | bytes 1179656 | tf_op jit(solution)/shard_map/ppermute | solution.py:12
  168.6 6.3 %copy-start.29 = (pred[256]{0:T(512)(128)(4,1)}, pred[256]{0:T(512)(128)(4,1)S(1)}, u32[]{:S(2)}) copy-start(pred[256]{0:T(512)(128)(4,1)S(1)} %iota_compare_fusion.1) | copy-start | bytes 772
  176.9 24.5 %copy-start.22 = (f32[1,1,3072]{2,1,0:T(1,128)S(1)}, f32[1,1,3072]{2,1,0:T(1,128)}, u32[]{:S(2)}) copy-start(f32[1,1,3072]{2,1,0:T(1,128)} %copy-done.20) | copy-start | bytes 36868
  176.9 60.8 %all-gather.19.cloned.1.call-start = ((), (), s32[]{:S(2)}) async-start(), calls=%async_computation.5 | async-start | bytes 1310720 | tf_op jit(solution)/shard_map/all_gather | solution.py:107
  201.4 6.7 %copy-start.30 = (pred[256]{0:T(512)(128)(4,1)S(1)}, pred[256]{0:T(512)(128)(4,1)}, u32[]{:S(2)}) copy-start(pred[256]{0:T(512)(128)(4,1)} %copy-done.29) | copy-start | bytes 772
  220.2 17.5 %copy-start.18 = (bf16[256,768]{1,0:T(8,128)(2,1)S(1)}, bf16[256,768]{1,0:T(8,128)(2,1)}, u32[]{:S(2)}) copy-start(bf16[256,768]{1,0:T(8,128)(2,1)} %fusion.111) | copy-start | bytes 1179652
  221.8 54.1 %all-gather.21.cloned.1.call-start = ((), (), s32[]{:S(2)}) async-start(), calls=%async_computation.6 | async-start | bytes 1966080 | tf_op jit(solution)/shard_map/all_gather | solution.py:125
  240.7 12.5 %collective-permute-start.2 = (bf16[256,768]{1,0:T(8,128)(2,1)}, bf16[256,768]{1,0:T(8,128)(2,1)S(1)}, u32[]{:S(2)}, u32[]{:S(2)}) collective-permute-start(bf16[256,768]{1,0:T(8,128)(2,1)} %select_convert_fusion.1), channel_id=1, source_target_pairs={{0,4},{4,8},{8,12},{1,5},{5,9},{9,13},{2,6},{6,10},{10,14},{3,7},{... | collective-permute-start | bytes 1179656 | tf_op jit(solution)/shard_map/ppermute | solution.py:12
  246.8 6.4 %copy-start.24 = (pred[256]{0:T(512)(128)(4,1)}, pred[256]{0:T(512)(128)(4,1)S(1)}, u32[]{:S(2)}) copy-start(pred[256]{0:T(512)(128)(4,1)S(1)} %iota_compare_fusion) | copy-start | bytes 772
  255.1 24.6 %copy-start.23 = (f32[1,1,3072]{2,1,0:T(1,128)S(1)}, f32[1,1,3072]{2,1,0:T(1,128)}, u32[]{:S(2)}) copy-start(f32[1,1,3072]{2,1,0:T(1,128)} %copy-done.20) | copy-start | bytes 36868
  255.1 61.0 %all-gather.23.cloned.1.call-start = ((), (), s32[]{:S(2)}) async-start(), calls=%async_computation.7 | async-start | bytes 1310720 | tf_op jit(solution)/shard_map/all_gather | solution.py:107
  279.7 6.7 %copy-start.25 = (pred[256]{0:T(512)(128)(4,1)S(1)}, pred[256]{0:T(512)(128)(4,1)}, u32[]{:S(2)}) copy-start(pred[256]{0:T(512)(128)(4,1)} %copy-done.24) | copy-start | bytes 772
  298.3 17.7 %copy-start.16 = (bf16[256,768]{1,0:T(8,128)(2,1)S(1)}, bf16[256,768]{1,0:T(8,128)(2,1)}, u32[]{:S(2)}) copy-start(bf16[256,768]{1,0:T(8,128)(2,1)} %fusion.113) | copy-start | bytes 1179652
  298.3 17.7 %copy-start.26 = (pred[256]{0:T(512)(128)(4,1)S(1)}, pred[256]{0:T(512)(128)(4,1)}, u32[]{:S(2)}) copy-start(pred[256]{0:T(512)(128)(4,1)} %copy-done.24) | copy-start | bytes 772
  (11 other events, 24.7 us)
Sparse Core Ops, SparseCore 0:
  14.5 22.3 all-gather.8
  59.8 20.3 all-gather.10
  97.8 20.5 all-gather.12
  142.7 16.7 all-gather.14
  177.0 20.5 all-gather.16
  221.9 15.7 all-gather.18
  255.2 20.6 all-gather.20
  300.0 15.9 all-gather.22
where the time goes:
time: 330 us; the launch traced here: 328 us
  waiting for transfers between devices  144 us (44%)
  local copies, waits for them, and re-layouts  55.7 us (17%)
  matrix products  48.4 us (15%)
  other arithmetic  39.2 us (12%)
  between operations  29.6 us (9%)
  starting transfers between devices  10.9 us (3%)
    all_gather x4, waiting for transfers between devices, gather_heads(): every_head = lax.all_gather(head_rows, 'seq', axis=1, tiled=True)  68.6 us
    all_gather x4, waiting for transfers between devices, shards(): full_rows = lax.all_gather(own_rows, 'seq', axis=1, tiled=True)  56.1 us
    dot_general x4, matrix products, run_block(): jnp.dot(shaped, qkv_weights, preferred_element_type=jnp.float32)  22.4 us
    unnamed x67, local copies, waits for them, and re-layouts  20.5 us
    ppermute x3, waiting for transfers between devices, passed_along(): lax.ppermute(value, axis, [(source, source + steps) for source in range(l...  19 us
    dynamic_update_slice x4, local copies, waits for them, and re-layouts, run_block(): lax.dynamic_update_slice_in_dim(value_cache, jnp.where(mask, fresh_values...  15.2 us
    dynamic_update_slice x4, local copies, waits for them, and re-layouts, run_block(): lax.dynamic_update_slice_in_dim(key_cache, jnp.where(mask, fresh_keys, wi...  14.8 us
    dot_general x4, matrix products, gather_heads(): return jnp.dot(every_head, out_weights, preferred_element_type=jnp.float32)  11.3 us
  transfers between devices with their start and end apart: 11, of which 10 were waited for; matrix products, arithmetic and copies ran while one was open for 7% of the time, Pallas kernels for 0%

commit v1 on v0

--- a/solution.py
+++ b/solution.py
@@ -104,7 +104,33 @@
     row_numbers = jnp.arange(biggest_patch_span)
 
     def gather_heads(head_rows):
-        every_head = lax.all_gather(head_rows, "seq", axis=1, tiled=True)
+
+        def clear_streams_on_mesh(vals, ax_name):
+            current_arr = lax.axis_size(ax_name)
+            found_now = lax.axis_index(ax_name)
+            piece_next, newest, piece_now = (current_arr, found_now, vals.shape[1])
+            fresh = jnp.zeros(
+                [j0 * piece_next if pp == 1 else j0 for pp, j0 in enumerate(vals.shape)], vals.dtype
+            )
+            front = lax.dynamic_update_slice_in_dim(fresh, vals, newest * piece_now, axis=1)
+            oldest = arr_now = vals
+            for hop_no in range(1, piece_next // 2 + 1):
+                oldest = lax.ppermute(
+                    oldest, ax_name, [(pp, (pp + 1) % piece_next) for pp in range(piece_next)]
+                )
+                front = lax.dynamic_update_slice_in_dim(
+                    front, oldest, (newest - hop_no) % piece_next * piece_now, axis=1
+                )
+                if 2 * hop_no < piece_next:
+                    arr_now = lax.ppermute(
+                        arr_now, ax_name, [(pp, (pp - 1) % piece_next) for pp in range(piece_next)]
+                    )
+                    front = lax.dynamic_update_slice_in_dim(
+                        front, arr_now, (newest + hop_no) % piece_next * piece_now, axis=1
+                    )
+            return front
+
+        every_head = clear_streams_on_mesh(head_rows, "seq")
         return jnp.dot(every_head, out_weights, preferred_element_type=jnp.float32)
 
     results = []

time: 330 us -> 309 us (0.936)
  waiting for transfers between devices: 144 us -> 112 us
  starting transfers between devices: 10.9 us -> 23.4 us
  matrix products: 48.4 us -> 43.5 us
  local copies, waits for them, and re-layouts: 55.7 us -> 59.5 us
    all_gather x4 -> x0, waiting for transfers between devices: 68.6 us -> none  [gather_heads(): every_head = lax.all_gather(head_rows, 'seq', axis=1, tiled=True)]
    ppermute x0 -> x12, waiting for transfers between devices: none -> 39.9 us  [the longest x8 39.9 us: clear_streams_on_mesh(): lax.ppermute(oldest, ax_name, [(pp, (pp + 1) % piece_next) for pp in rang...]
    ppermute x0 -> x12, starting transfers between devices: none -> 10.3 us  [the longest x4 6.48 us: clear_streams_on_mesh(): lax.ppermute(arr_now, ax_name, [(pp, (pp - 1) % piece_next) for pp in ran...]
    ppermute x3, waiting for transfers between devices: 19 us -> 11.2 us  [passed_along(): lax.ppermute(value, axis, [(source, source + steps) for source in range(l...]
    dot_general x4, matrix products: 11.3 us -> 4.88 us  [gather_heads(): return jnp.dot(every_head, out_weights, preferred_element_type=jnp.float32)]
    all_gather x4, waiting for transfers between devices: 56.1 us -> 61.1 us  [shards(): full_rows = lax.all_gather(own_rows, 'seq', axis=1, tiled=True)]
    unnamed x67 -> x79, local copies, waits for them, and re-layouts: 20.5 us -> 20.6 us
  transfers between devices with their start and end apart: 11 -> 19, of which waited for: 10 -> 14; matrix products, arithmetic and copies ran while one was open for 7% -> 9% of each run, Pallas kernels for 0% -> 0%
where the time goes in v1:
time: 309 us; the launch traced here: 307 us
  waiting for transfers between devices  112 us (36%)
  local copies, waits for them, and re-layouts  59.5 us (19%)
  matrix products  43.5 us (14%)
  other arithmetic  38.8 us (13%)
  between operations  29.6 us (10%)
  starting transfers between devices  23.4 us (8%)
    all_gather x4, waiting for transfers between devices, shards(): full_rows = lax.all_gather(own_rows, 'seq', axis=1, tiled=True)  61.1 us
    ppermute x8, waiting for transfers between devices, clear_streams_on_mesh(): lax.ppermute(oldest, ax_name, [(pp, (pp + 1) % piece_next) for pp in rang...  39.9 us
    dot_general x4, matrix products, run_block(): jnp.dot(shaped, qkv_weights, preferred_element_type=jnp.float32)  22.4 us
    unnamed x79, local copies, waits for them, and re-layouts  20.6 us
    dynamic_update_slice x4, local copies, waits for them, and re-layouts, run_block(): lax.dynamic_update_slice_in_dim(value_cache, jnp.where(mask, fresh_values...  15.1 us
    dynamic_update_slice x4, local copies, waits for them, and re-layouts, run_block(): lax.dynamic_update_slice_in_dim(key_cache, jnp.where(mask, fresh_keys, wi...  15 us
    ppermute x3, starting transfers between devices, passed_along(): lax.ppermute(value, axis, [(source, source + steps) for source in range(l...  12.7 us
    ppermute x3, waiting for transfers between devices, passed_along(): lax.ppermute(value, axis, [(source, source + steps) for source in range(l...  11.2 us
  transfers between devices with their start and end apart: 19, of which 14 were waited for; matrix products, arithmetic and copies ran while one was open for 9% of the time, Pallas kernels for 0%

profile of v1, /device:TPU:0, one launch (start us, length us, event | category | flops | bytes accessed | tf_op | source)
XLA Modules:
  0.0 307.0 jit_solution(11014535421936634107)
XLA Ops:
  15.8 12.7 %copy.33 = bf16[1,3072,1536]{1,2,0:T(8,128)(2,1)} copy(bf16[1,3072,1536]{2,1,0:T(8,128)(2,1)} %param.14) | data formatting | bytes 18874368 | tf_op args[5]
  42.3 5.7 %fusion.37 = f32[256,4,3,128]{0,3,2,1:T(8,128)S(1)} fusion(bf16[4,3,128,3072]{3,2,1,0:T(8,128)(2,1)} %bitcast.227, bf16[256,3072]{1,0:T(8,128)(2,1)S(1)} %copy-done.3, f32[3072]{0:T(1024)S(1)} %bitcast.250, f32[3072]{0:T(1024)S(1)} %bitcast.246, f32[256]{0:T(256)S(1)} %add_rsqrt_fusion.11, f32[256]{0:T(256)S(1)} %broadcast_multiply_fusion.3), kind=kOutput, calls=%fused_computation.57 | convolution fusion | flops 2420637696 | bytes 12609536 | tf_op jit(solution)/shard_map/dot_general | solution.py:49
  49.3 3.5 %dynamic_update_slice.73 = bf16[4,1024,128]{1,2,0:T(8,128)(2,1)} dynamic-update-slice(bf16[4,1024,128]{1,2,0:T(8,128)(2,1)} %concatenate.11, bf16[4,256,128]{1,2,0:T(8,128)(2,1)} %get-tuple-element.29, s32[]{:T(128)} %constant.95.clone.1, s32[]{:T(128)S(6)} %select_n.212, s32[]{:T(128)} %constant.95.clone.1) | dynamic-update-slice | bytes 524292 | tf_op jit(solution)/shard_map/dynamic_update_slice | solution.py:57
  52.7 3.6 %fusion.32 = (f32[4,256]{1,0:T(4,128)S(1)}, f32[4,256,768]{2,1,0:T(8,128)}) fusion(bf16[4,1024,128]{1,2,0:T(8,128)(2,1)} %dynamic_update_slice.73, f32[256,4,3,128]{0,3,2,1:T(8,128)} %copy-done.8, f32[256,4]{0,1:T(4,128)S(1)} %get-tuple-element.44), kind=kOutput, calls=%fused_computation.48 | convolution fusion | flops 203160576 | bytes 4464640 | tf_op jit(solution)/shard_map/qhd,hkd->hqk/dot_general | solution.py:64
  56.4 3.4 %dynamic_update_slice.72 = bf16[4,1024,128]{1,2,0:T(8,128)(2,1)} dynamic-update-slice(bf16[4,1024,128]{1,2,0:T(8,128)(2,1)} %concatenate.10, bf16[4,256,128]{1,2,0:T(8,128)(2,1)S(1)} %get-tuple-element.28, s32[]{:T(128)} %constant.95.clone.1, s32[]{:T(128)S(6)} %select_n.212, s32[]{:T(128)} %constant.95.clone.1) | dynamic-update-slice | bytes 524292 | tf_op jit(solution)/shard_map/dynamic_update_slice | solution.py:61
  59.8 3.6 %fusion.122 = bf16[4,128,256]{2,1,0:T(8,128)(2,1)} fusion(f32[4,256,768]{2,1,0:T(8,128)} %get-tuple-element.36, f32[4,256]{1,0:T(4,128)S(1)} %get-tuple-element.35, bf16[4,1024,128]{1,2,0:T(8,128)(2,1)} %dynamic_update_slice.72), kind=kOutput, calls=%fused_computation.105 | convolution fusion | flops 203816960 | bytes 4198400 | tf_op jit(solution)/shard_map/hqk,hkd->qhd/dot_general | solution.py:69
  66.5 3.8 %collective-permute-done = bf16[256,512]{0,1:T(8,128)(2,1)} collective-permute-done((bf16[256,512]{0,1:T(8,128)(2,1)}, bf16[256,512]{0,1:T(8,128)(2,1)}, u32[]{:S(2)}, u32[]{:S(2)}) %collective-permute-start) | collective-permute-done | bytes 262176 | tf_op jit(solution)/shard_map/ppermute | solution.py:118
  70.3 2.6 collective-permute-start.2
  78.1 5.9 %collective-permute-start.3 = (bf16[256,768]{1,0:T(8,128)(2,1)}, bf16[256,768]{1,0:T(8,128)(2,1)S(1)}, u32[]{:S(2)}, u32[]{:S(2)}) collective-permute-start(bf16[256,768]{1,0:T(8,128)(2,1)} %fusion.104), channel_id=1, source_target_pairs={{0,4},{4,8},{8,12},{1,5},{5,9},{9,13},{2,6},{6,10},{10,14},{3,7},{... | collective-permute-start | bytes 1179656 | tf_op jit(solution)/shard_map/ppermute | solution.py:12
  86.7 6.5 %collective-permute-done.3 = bf16[256,768]{1,0:T(8,128)(2,1)S(1)} collective-permute-done((bf16[256,768]{1,0:T(8,128)(2,1)}, bf16[256,768]{1,0:T(8,128)(2,1)S(1)}, u32[]{:S(2)}, u32[]{:S(2)}) %collective-permute-start.3) | collective-permute-done | bytes 393248 | tf_op jit(solution)/shard_map/ppermute | solution.py:12
  97.2 19.0 %all-gather.7.cloned.1.call-done = bf16[256,3072]{1,0:T(8,128)(2,1)} async-done(((bf16[256,768]{1,0:T(8,128)(2,1)}), bf16[256,3072]{1,0:T(8,128)(2,1)}) %all-gather.7.cloned.1.call-update) | async-done | bytes 1572880 | tf_op jit(solution)/shard_map/all_gather | solution.py:151
  120.0 5.6 %fusion.40 = f32[256,4,3,128]{0,3,2,1:T(8,128)S(1)} fusion(bf16[4,3,128,3072]{3,2,1,0:T(8,128)(2,1)} %bitcast.228, bf16[256,3072]{1,0:T(8,128)(2,1)S(1)} %copy-done.5, f32[256]{0:T(256)S(1)} %add_rsqrt_fusion.10, f32[256]{0:T(256)S(1)} %broadcast_multiply_fusion.2, f32[3072]{0:T(1024)S(1)} %bitcast.251, f32[3072]{0:T(1024)S(1)} %bitcast.247), kind=kOutput, calls=%fused_computation.59 | convolution fusion | flops 2420637696 | bytes 12609536 | tf_op jit(solution)/shard_map/dot_general | solution.py:49
  128.8 3.9 %dynamic_update_slice.79 = bf16[4,1024,128]{1,2,0:T(8,128)(2,1)} dynamic-update-slice(bf16[4,1024,128]{1,2,0:T(8,128)(2,1)} %dynamic_update_slice.73, bf16[4,256,128]{1,2,0:T(8,128)(2,1)} %get-tuple-element.27, s32[]{:T(128)} %constant.95.clone.1, s32[]{:T(128)S(6)} %select_n.229, s32[]{:T(128)} %constant.95.clone.1) | dynamic-update-slice | bytes 524292 | tf_op jit(solution)/shard_map/dynamic_update_slice | solution.py:57
  132.8 3.9 %dynamic_update_slice.78 = bf16[4,1024,128]{1,2,0:T(8,128)(2,1)} dynamic-update-slice(bf16[4,1024,128]{1,2,0:T(8,128)(2,1)} %dynamic_update_slice.72, bf16[4,256,128]{1,2,0:T(8,128)(2,1)S(1)} %get-tuple-element.26, s32[]{:T(128)} %constant.95.clone.1, s32[]{:T(128)S(6)} %select_n.229, s32[]{:T(128)} %constant.95.clone.1) | dynamic-update-slice | bytes 524292 | tf_op jit(solution)/shard_map/dynamic_update_slice | solution.py:61
  141.4 6.3 %collective-permute-done.4 = bf16[256,512]{0,1:T(8,128)(2,1)S(1)} collective-permute-done((bf16[256,512]{0,1:T(8,128)(2,1)S(1)}, bf16[256,512]{0,1:T(8,128)(2,1)S(1)}, u32[]{:S(2)}, u32[]{:S(2)}) %collective-permute-start.4) | collective-permute-done | bytes 262176 | tf_op jit(solution)/shard_map/ppermute | solution.py:118
  147.9 5.6 %collective-permute-done.6 = bf16[256,512]{0,1:T(8,128)(2,1)S(1)} collective-permute-done((bf16[256,512]{0,1:T(8,128)(2,1)S(1)}, bf16[256,512]{0,1:T(8,128)(2,1)S(1)}, u32[]{:S(2)}, u32[]{:S(2)}) %collective-permute-start.6) | collective-permute-done | bytes 262176 | tf_op jit(solution)/shard_map/ppermute | solution.py:118
  154.6 3.0 collective-permute-start.7
  166.6 21.8 %all-gather.9.cloned.1.call-done = bf16[256,3072]{1,0:T(8,128)(2,1)} async-done(((bf16[256,768]{1,0:T(8,128)(2,1)}), bf16[256,3072]{1,0:T(8,128)(2,1)}) %all-gather.9.cloned.1.call-update) | async-done | bytes 1572880 | tf_op jit(solution)/shard_map/all_gather | solution.py:151
  192.2 5.6 %fusion.43 = f32[256,4,3,128]{0,3,2,1:T(8,128)S(1)} fusion(bf16[4,3,128,3072]{3,2,1,0:T(8,128)(2,1)} %bitcast.229, bf16[256,3072]{1,0:T(8,128)(2,1)S(1)} %copy-done.6, f32[256]{0:T(256)S(1)} %add_rsqrt_fusion.9, f32[256]{0:T(256)S(1)} %broadcast_multiply_fusion.1, f32[3072]{0:T(1024)S(1)} %bitcast.252, f32[3072]{0:T(1024)S(1)} %bitcast.248), kind=kOutput, calls=%fused_computation.61 | convolution fusion | flops 2420637696 | bytes 12609536 | tf_op jit(solution)/shard_map/dot_general | solution.py:49
  201.1 3.9 %dynamic_update_slice.85 = bf16[4,1024,128]{1,2,0:T(8,128)(2,1)} dynamic-update-slice(bf16[4,1024,128]{1,2,0:T(8,128)(2,1)} %dynamic_update_slice.79, bf16[4,256,128]{1,2,0:T(8,128)(2,1)} %get-tuple-element.25, s32[]{:T(128)} %constant.95.clone.1, s32[]{:T(128)S(6)} %select_n.239, s32[]{:T(128)} %constant.95.clone.1) | dynamic-update-slice | bytes 524292 | tf_op jit(solution)/shard_map/dynamic_update_slice | solution.py:57
  205.0 3.9 %dynamic_update_slice.84 = bf16[4,1024,128]{1,2,0:T(8,128)(2,1)} dynamic-update-slice(bf16[4,1024,128]{1,2,0:T(8,128)(2,1)} %dynamic_update_slice.78, bf16[4,256,128]{1,2,0:T(8,128)(2,1)S(1)} %get-tuple-element.24, s32[]{:T(128)} %constant.95.clone.1, s32[]{:T(128)S(6)} %select_n.239, s32[]{:T(128)} %constant.95.clone.1) | dynamic-update-slice | bytes 524292 | tf_op jit(solution)/shard_map/dynamic_update_slice | solution.py:61
  213.7 6.3 %collective-permute-done.8 = bf16[256,512]{0,1:T(8,128)(2,1)S(1)} collective-permute-done((bf16[256,512]{0,1:T(8,128)(2,1)S(1)}, bf16[256,512]{0,1:T(8,128)(2,1)S(1)}, u32[]{:S(2)}, u32[]{:S(2)}) %collective-permute-start.8) | collective-permute-done | bytes 262176 | tf_op jit(solution)/shard_map/ppermute | solution.py:118
  220.2 5.6 %collective-permute-done.10 = bf16[256,512]{0,1:T(8,128)(2,1)S(1)} collective-permute-done((bf16[256,512]{0,1:T(8,128)(2,1)S(1)}, bf16[256,512]{0,1:T(8,128)(2,1)S(1)}, u32[]{:S(2)}, u32[]{:S(2)}) %collective-permute-start.10) | collective-permute-done | bytes 262176 | tf_op jit(solution)/shard_map/ppermute | solution.py:118
  226.9 3.8 %collective-permute-start.11 = (bf16[256,768]{1,0:T(8,128)(2,1)S(1)}, bf16[256,768]{1,0:T(8,128)(2,1)}, u32[]{:S(2)}, u32[]{:S(2)}) collective-permute-start(bf16[256,768]{1,0:T(8,128)(2,1)S(1)} %fusion.110), channel_id=1, source_target_pairs={{0,4},{4,8},{8,12},{1,5},{5,9},{9,13},{2,6},{6,10},{10,14},{3,7},{... | collective-permute-start | bytes 1179656 | tf_op jit(solution)/shard_map/ppermute | solution.py:12
  233.2 2.5 collective-permute-done.11
  239.5 20.3 %all-gather.11.cloned.1.call-done = bf16[256,3072]{1,0:T(8,128)(2,1)} async-done(((bf16[256,768]{1,0:T(8,128)(2,1)}), bf16[256,3072]{1,0:T(8,128)(2,1)}) %all-gather.11.cloned.1.call-update) | async-done | bytes 1572880 | tf_op jit(solution)/shard_map/all_gather | solution.py:151
  263.6 5.6 %fusion.46 = f32[256,4,3,128]{0,3,2,1:T(8,128)S(1)} fusion(bf16[4,3,128,3072]{3,2,1,0:T(8,128)(2,1)} %bitcast.230, bf16[256,3072]{1,0:T(8,128)(2,1)S(1)} %copy-done.4, f32[256]{0:T(256)S(1)} %add_rsqrt_fusion.8, f32[256]{0:T(256)S(1)} %broadcast_multiply_fusion, f32[3072]{0:T(1024)S(1)} %bitcast.253, f32[3072]{0:T(1024)S(1)} %bitcast.249), kind=kOutput, calls=%fused_computation.63 | convolution fusion | flops 2420637696 | bytes 12609536 | tf_op jit(solution)/shard_map/dot_general | solution.py:49
  272.4 3.9 %dynamic_update_slice.90 = bf16[4,1024,128]{1,2,0:T(8,128)(2,1)} dynamic-update-slice(bf16[4,1024,128]{1,2,0:T(8,128)(2,1)} %dynamic_update_slice.84, bf16[4,256,128]{1,2,0:T(8,128)(2,1)} %get-tuple-element.18, s32[]{:T(128)} %constant.95.clone.1, s32[]{:T(128)S(6)} %select_n.249, s32[]{:T(128)} %constant.95.clone.1) | dynamic-update-slice | bytes 524292 | tf_op jit(solution)/shard_map/dynamic_update_slice | solution.py:61
  276.3 3.8 %dynamic_update_slice.91 = bf16[4,1024,128]{1,2,0:T(8,128)(2,1)} dynamic-update-slice(bf16[4,1024,128]{1,2,0:T(8,128)(2,1)} %dynamic_update_slice.85, bf16[4,256,128]{1,2,0:T(8,128)(2,1)S(1)} %get-tuple-element.19, s32[]{:T(128)} %constant.95.clone.1, s32[]{:T(128)S(6)} %select_n.249, s32[]{:T(128)} %constant.95.clone.1) | dynamic-update-slice | bytes 524292 | tf_op jit(solution)/shard_map/dynamic_update_slice | solution.py:57
  284.8 6.3 %collective-permute-done.12 = bf16[256,512]{0,1:T(8,128)(2,1)S(1)} collective-permute-done((bf16[256,512]{0,1:T(8,128)(2,1)S(1)}, bf16[256,512]{0,1:T(8,128)(2,1)S(1)}, u32[]{:S(2)}, u32[]{:S(2)}) %collective-permute-start.12) | collective-permute-done | bytes 262176 | tf_op jit(solution)/shard_map/ppermute | solution.py:118
  291.3 5.6 %collective-permute-done.14 = bf16[256,512]{0,1:T(8,128)(2,1)S(1)} collective-permute-done((bf16[256,512]{0,1:T(8,128)(2,1)S(1)}, bf16[256,512]{0,1:T(8,128)(2,1)S(1)}, u32[]{:S(2)}, u32[]{:S(2)}) %collective-permute-start.14) | collective-permute-done | bytes 262176 | tf_op jit(solution)/shard_map/ppermute | solution.py:118
  298.1 2.3 maximum_bitcast_fusion
  (183 shorter events, 77.7 us)
Async XLA Ops:
  6.5 69.8 %copy-start = (bf16[1,2048,768]{2,1,0:T(8,128)(2,1)S(1)}, bf16[1,2048,768]{2,1,0:T(8,128)(2,1)}, u32[]{:S(2)}) copy-start(bf16[1,2048,768]{2,1,0:T(8,128)(2,1)} %param.15) | copy-start | bytes 9437188
  6.5 32.0 %all-gather.5.cloned.1.call-start = ((), (), s32[]{:S(2)}) async-start(), calls=%async_computation | async-start | bytes 1966080 | tf_op jit(solution)/shard_map/all_gather | solution.py:151
  11.7 36.5 %copy-start.36 = (pred[256]{0:T(512)(128)(4,1)}, pred[256]{0:T(512)(128)(4,1)S(1)}, u32[]{:S(2)}) copy-start(pred[256]{0:T(512)(128)(4,1)S(1)} %iota_compare_fusion.3) | copy-start | bytes 772
  14.5 101.7 %all-gather.7.cloned.1.call-start = ((), (), s32[]{:S(2)}) async-start(), calls=%async_computation.1 | async-start | bytes 1966080 | tf_op jit(solution)/shard_map/all_gather | solution.py:151
  63.4 12.9 %copy-start.14 = (bf16[256,768]{1,0:T(8,128)(2,1)S(1)}, bf16[256,768]{1,0:T(8,128)(2,1)}, u32[]{:S(2)}) copy-start(bf16[256,768]{1,0:T(8,128)(2,1)} %fusion.136) | copy-start | bytes 1179652
  63.4 6.9 %collective-permute-start = (bf16[256,512]{0,1:T(8,128)(2,1)}, bf16[256,512]{0,1:T(8,128)(2,1)}, u32[]{:S(2)}, u32[]{:S(2)}) collective-permute-start(bf16[256,512]{0,1:T(8,128)(2,1)} %bitcast.19), channel_id=1, source_target_pairs={{0,1},{1,2},{2,3},{3,0},{4,5},{5,6},{6,7},{7,4},{8,9},{9,10},{10,1... | collective-permute-start | bytes 786440 | tf_op jit(solution)/shard_map/ppermute | solution.py:118
  63.8 11.1 %collective-permute-start.1 = (bf16[256,512]{0,1:T(8,128)(2,1)}, bf16[256,512]{0,1:T(8,128)(2,1)}, u32[]{:S(2)}, u32[]{:S(2)}) collective-permute-start(bf16[256,512]{0,1:T(8,128)(2,1)} %bitcast.19), channel_id=1, source_target_pairs={{0,3},{1,0},{2,1},{3,2},{4,7},{5,4},{6,5},{7,6},{8,11},{9,8},{10,9... | collective-permute-start | bytes 786440 | tf_op jit(solution)/shard_map/ppermute | solution.py:125
  66.5 9.9 %copy-start.37 = (pred[256]{0:T(512)(128)(4,1)S(1)}, pred[256]{0:T(512)(128)(4,1)}, u32[]{:S(2)}) copy-start(pred[256]{0:T(512)(128)(4,1)} %copy-done.36) | copy-start | bytes 772
  70.3 6.0 %collective-permute-start.2 = (bf16[256,512]{0,1:T(8,128)(2,1)}, bf16[256,512]{0,1:T(8,128)(2,1)S(1)}, u32[]{:S(2)}, u32[]{:S(2)}) collective-permute-start(bf16[256,512]{0,1:T(8,128)(2,1)} %collective-permute-done), channel_id=1, source_target_pairs={{0,1},{1,2},{2,3},{3,0},{4,5},{5,6},{6,7},{7,4},{8,9},{9,10},{10,1... | collective-permute-start | bytes 786440 | tf_op jit(solution)/shard_map/ppermute | solution.py:118
  78.1 15.0 %collective-permute-start.3 = (bf16[256,768]{1,0:T(8,128)(2,1)}, bf16[256,768]{1,0:T(8,128)(2,1)S(1)}, u32[]{:S(2)}, u32[]{:S(2)}) collective-permute-start(bf16[256,768]{1,0:T(8,128)(2,1)} %fusion.104), channel_id=1, source_target_pairs={{0,4},{4,8},{8,12},{1,5},{5,9},{9,13},{2,6},{6,10},{10,14},{3,7},{... | collective-permute-start | bytes 1179656 | tf_op jit(solution)/shard_map/ppermute | solution.py:12
  95.1 24.9 %copy-start.24 = (f32[1,1,3072]{2,1,0:T(1,128)S(1)}, f32[1,1,3072]{2,1,0:T(1,128)}, u32[]{:S(2)}) copy-start(f32[1,1,3072]{2,1,0:T(1,128)} %copy-done.23) | copy-start | bytes 36868
  95.1 93.3 %all-gather.9.cloned.1.call-start = ((), (), s32[]{:S(2)}) async-start(), calls=%async_computation.2 | async-start | bytes 1966080 | tf_op jit(solution)/shard_map/all_gather | solution.py:151
  139.6 13.9 %copy-start.16 = (bf16[256,768]{1,0:T(8,128)(2,1)S(1)}, bf16[256,768]{1,0:T(8,128)(2,1)}, u32[]{:S(2)}) copy-start(bf16[256,768]{1,0:T(8,128)(2,1)} %fusion.138) | copy-start | bytes 1179652
  139.6 13.9 %copy-start.32 = (pred[256]{0:T(512)(128)(4,1)S(1)}, pred[256]{0:T(512)(128)(4,1)}, u32[]{:S(2)}) copy-start(pred[256]{0:T(512)(128)(4,1)} %copy-done.30) | copy-start | bytes 772
  139.6 8.1 %collective-permute-start.4 = (bf16[256,512]{0,1:T(8,128)(2,1)S(1)}, bf16[256,512]{0,1:T(8,128)(2,1)S(1)}, u32[]{:S(2)}, u32[]{:S(2)}) collective-permute-start(bf16[256,512]{0,1:T(8,128)(2,1)S(1)} %bitcast.240), channel_id=1, source_target_pairs={{0,1},{1,2},{2,3},{3,0},{4,5},{5,6},{6,7},{7,4},{8,9},{9,10},{10,1... | collective-permute-start | bytes 786440 | tf_op jit(solution)/shard_map/ppermute | solution.py:118
  139.9 7.9 %collective-permute-start.5 = (bf16[256,512]{0,1:T(8,128)(2,1)S(1)}, bf16[256,512]{0,1:T(8,128)(2,1)S(1)}, u32[]{:S(2)}, u32[]{:S(2)}) collective-permute-start(bf16[256,512]{0,1:T(8,128)(2,1)S(1)} %bitcast.241), channel_id=1, source_target_pairs={{0,3},{1,0},{2,1},{3,2},{4,7},{5,4},{6,5},{7,6},{8,11},{9,8},{10,9... | collective-permute-start | bytes 786440 | tf_op jit(solution)/shard_map/ppermute | solution.py:125
  147.7 5.8 %collective-permute-start.6 = (bf16[256,512]{0,1:T(8,128)(2,1)S(1)}, bf16[256,512]{0,1:T(8,128)(2,1)S(1)}, u32[]{:S(2)}, u32[]{:S(2)}) collective-permute-start(bf16[256,512]{0,1:T(8,128)(2,1)S(1)} %collective-permute-done.4), channel_id=1, source_target_pairs={{0,1},{1,2},{2,3},{3,0},{4,5},{5,6},{6,7},{7,4},{8,9},{9,10},{10,1... | collective-permute-start | bytes 786440 | tf_op jit(solution)/shard_map/ppermute | solution.py:118
  154.6 43.2 %copy-start.18 = (bf16[256,768]{1,0:T(8,128)(2,1)}, bf16[256,768]{1,0:T(8,128)(2,1)S(1)}, u32[]{:S(2)}) copy-start(bf16[256,768]{1,0:T(8,128)(2,1)S(1)} %fusion.107) | copy-start | bytes 1179652
  154.6 7.9 %collective-permute-start.7 = (bf16[256,768]{1,0:T(8,128)(2,1)S(1)}, bf16[256,768]{1,0:T(8,128)(2,1)}, u32[]{:S(2)}, u32[]{:S(2)}) collective-permute-start(bf16[256,768]{1,0:T(8,128)(2,1)S(1)} %fusion.107), channel_id=1, source_target_pairs={{0,4},{4,8},{8,12},{1,5},{5,9},{9,13},{2,6},{6,10},{10,14},{3,7},{... | collective-permute-start | bytes 1179656 | tf_op jit(solution)/shard_map/ppermute | solution.py:12
  164.5 95.2 %all-gather.11.cloned.1.call-start = ((), (), s32[]{:S(2)}) async-start(), calls=%async_computation.3 | async-start | bytes 1966080 | tf_op jit(solution)/shard_map/all_gather | solution.py:151
  211.9 13.9 %copy-start.17 = (bf16[256,768]{1,0:T(8,128)(2,1)S(1)}, bf16[256,768]{1,0:T(8,128)(2,1)}, u32[]{:S(2)}) copy-start(bf16[256,768]{1,0:T(8,128)(2,1)} %fusion.140) | copy-start | bytes 1179652
  211.9 13.9 %copy-start.35 = (pred[256]{0:T(512)(128)(4,1)S(1)}, pred[256]{0:T(512)(128)(4,1)}, u32[]{:S(2)}) copy-start(pred[256]{0:T(512)(128)(4,1)} %copy-done.33) | copy-start | bytes 772
  211.9 8.1 %collective-permute-start.8 = (bf16[256,512]{0,1:T(8,128)(2,1)S(1)}, bf16[256,512]{0,1:T(8,128)(2,1)S(1)}, u32[]{:S(2)}, u32[]{:S(2)}) collective-permute-start(bf16[256,512]{0,1:T(8,128)(2,1)S(1)} %bitcast.243), channel_id=1, source_target_pairs={{0,1},{1,2},{2,3},{3,0},{4,5},{5,6},{6,7},{7,4},{8,9},{9,10},{10,1... | collective-permute-start | bytes 786440 | tf_op jit(solution)/shard_map/ppermute | solution.py:118
  212.2 7.9 %collective-permute-start.9 = (bf16[256,512]{0,1:T(8,128)(2,1)S(1)}, bf16[256,512]{0,1:T(8,128)(2,1)S(1)}, u32[]{:S(2)}, u32[]{:S(2)}) collective-permute-start(bf16[256,512]{0,1:T(8,128)(2,1)S(1)} %bitcast.244), channel_id=1, source_target_pairs={{0,3},{1,0},{2,1},{3,2},{4,7},{5,4},{6,5},{7,6},{8,11},{9,8},{10,9... | collective-permute-start | bytes 786440 | tf_op jit(solution)/shard_map/ppermute | solution.py:125
  220.0 5.8 %collective-permute-start.10 = (bf16[256,512]{0,1:T(8,128)(2,1)S(1)}, bf16[256,512]{0,1:T(8,128)(2,1)S(1)}, u32[]{:S(2)}, u32[]{:S(2)}) collective-permute-start(bf16[256,512]{0,1:T(8,128)(2,1)S(1)} %collective-permute-done.8), channel_id=1, source_target_pairs={{0,1},{1,2},{2,3},{3,0},{4,5},{5,6},{6,7},{7,4},{8,9},{9,10},{10,1... | collective-permute-start | bytes 786440 | tf_op jit(solution)/shard_map/ppermute | solution.py:118
  226.9 42.3 %copy-start.20 = (bf16[256,768]{1,0:T(8,128)(2,1)}, bf16[256,768]{1,0:T(8,128)(2,1)S(1)}, u32[]{:S(2)}) copy-start(bf16[256,768]{1,0:T(8,128)(2,1)S(1)} %fusion.110) | copy-start | bytes 1179652
  226.9 8.8 %collective-permute-start.11 = (bf16[256,768]{1,0:T(8,128)(2,1)S(1)}, bf16[256,768]{1,0:T(8,128)(2,1)}, u32[]{:S(2)}, u32[]{:S(2)}) collective-permute-start(bf16[256,768]{1,0:T(8,128)(2,1)S(1)} %fusion.110), channel_id=1, source_target_pairs={{0,4},{4,8},{8,12},{1,5},{5,9},{9,13},{2,6},{6,10},{10,14},{3,7},{... | collective-permute-start | bytes 1179656 | tf_op jit(solution)/shard_map/ppermute | solution.py:12
  283.0 13.9 %copy-start.15 = (bf16[256,768]{1,0:T(8,128)(2,1)S(1)}, bf16[256,768]{1,0:T(8,128)(2,1)}, u32[]{:S(2)}) copy-start(bf16[256,768]{1,0:T(8,128)(2,1)} %fusion.142) | copy-start | bytes 1179652
  283.0 13.9 %copy-start.29 = (pred[256]{0:T(512)(128)(4,1)S(1)}, pred[256]{0:T(512)(128)(4,1)}, u32[]{:S(2)}) copy-start(pred[256]{0:T(512)(128)(4,1)} %copy-done.27) | copy-start | bytes 772
  283.0 8.1 %collective-permute-start.12 = (bf16[256,512]{0,1:T(8,128)(2,1)S(1)}, bf16[256,512]{0,1:T(8,128)(2,1)S(1)}, u32[]{:S(2)}, u32[]{:S(2)}) collective-permute-start(bf16[256,512]{0,1:T(8,128)(2,1)S(1)} %bitcast.237), channel_id=1, source_target_pairs={{0,1},{1,2},{2,3},{3,0},{4,5},{5,6},{6,7},{7,4},{8,9},{9,10},{10,1... | collective-permute-start | bytes 786440 | tf_op jit(solution)/shard_map/ppermute | solution.py:118
  283.3 7.9 %collective-permute-start.13 = (bf16[256,512]{0,1:T(8,128)(2,1)S(1)}, bf16[256,512]{0,1:T(8,128)(2,1)S(1)}, u32[]{:S(2)}, u32[]{:S(2)}) collective-permute-start(bf16[256,512]{0,1:T(8,128)(2,1)S(1)} %bitcast.238), channel_id=1, source_target_pairs={{0,3},{1,0},{2,1},{3,2},{4,7},{5,4},{6,5},{7,6},{8,11},{9,8},{10,9... | collective-permute-start | bytes 786440 | tf_op jit(solution)/shard_map/ppermute | solution.py:125
  291.1 5.8 %collective-permute-start.14 = (bf16[256,512]{0,1:T(8,128)(2,1)S(1)}, bf16[256,512]{0,1:T(8,128)(2,1)S(1)}, u32[]{:S(2)}, u32[]{:S(2)}) collective-permute-start(bf16[256,512]{0,1:T(8,128)(2,1)S(1)} %collective-permute-done.12), channel_id=1, source_target_pairs={{0,1},{1,2},{2,3},{3,0},{4,5},{5,6},{6,7},{7,4},{8,9},{9,10},{10,1... | collective-permute-start | bytes 786440 | tf_op jit(solution)/shard_map/ppermute | solution.py:118
  (25 other events, 98.8 us)
Sparse Core Ops, SparseCore 0:
  14.7 22.3 all-gather.4
  95.3 20.9 all-gather.6
  164.7 23.7 all-gather.8
  237.7 21.9 all-gather.10
